TPU v7x, 256 devices: a whole 4x4x8 slice. The times are simulated.
256 devices in a mesh: wide: 32 (over x, y, core), blk: 8 (over z).
Axes of the slice: x: 4, y: 4, z: 8, core: 2. Of those that a mesh axis runs over, the one named last changes fastest.
Arguments:
- tokens: bfloat16 [1024, 8192], P('wide', 'blk'), may hold values from -6 to 6
- target: bfloat16 [1024, 8192], P('wide', 'blk'), may hold values from -3 to 3
- probe_vector: float32 [8192], P('blk'), may hold values from -12 to 12
- weight_in: bfloat16 [256, 8, 2, 128, 128], P('wide', 'blk'), may hold values from -0.375 to 0.375
- weight_out: bfloat16 [256, 8, 2, 128, 128], P('wide', 'blk'), may hold values from -0.09375 to 0.09375
- slot_rows: int32 [256, 8, 2], P('wide', 'blk'), may hold values from 0 to 7, as said below
- slot_count: int32 [256, 8], P('wide', 'blk'), may hold values from 0 to 2, as said below
Outputs:
- outputs: bfloat16 [1024, 8192], P('wide', 'blk')
- token_grad: bfloat16 [1024, 8192], P('wide', 'blk')
- grad_in: float32 [256, 8, 2, 128, 128], P('wide', 'blk')
- grad_out: float32 [256, 8, 2, 128, 128], P('wide', 'blk')
Inputs may be any that keep to these rules, and one draw needn't show every extreme that they name: `slot_rows`: the 2 entries of one (j, g) are distinct feature blocks of the row group. `slot_count`: every hidden block column has 2 used slots in at least one row group.
All inputs are finite; a program needn't handle non-finite values.
Results may differ from a plain program's by a relative error of at most 0.033.
Values may be sent and summed in bfloat16 or wider, within the bound.
No kernel may reach another device: no remote copies, remote signals or barrier semaphores. Data moves between devices by JAX's collectives and lax.ppermute only.
A program may use at most 64 MiB of HBM per device.

v0:
```python
import jax
import jax.numpy as jnp
from jax import lax
from jax.sharding import Mesh, PartitionSpec as P

WIDE = ("chip", "core")


def activate(value):
    return jax.nn.gelu(value, approximate=True)


def activate_slope(value):
    return jax.jvp(activate, (value,), (jnp.ones_like(value),))[1]


def spread_tiles(tiles, row_index, feature_blocks):
    rows = lax.broadcasted_iota(jnp.int32, (feature_blocks,) + row_index.shape, 0)
    hit = rows == row_index[None]
    zero = jnp.zeros((), tiles.dtype)
    dense = jnp.where(hit[:, :, 0, None, None], tiles[None, :, 0], zero)
    for slot in range(1, row_index.shape[1]):
        dense = dense + jnp.where(hit[:, :, slot, None, None], tiles[None, :, slot], zero)
    return jnp.transpose(dense, (0, 2, 1, 3))


def pick_tiles(dense, row_index):
    feature_blocks = dense.shape[0]
    rows = lax.broadcasted_iota(jnp.int32, (feature_blocks,) + row_index.shape, 0)
    hit = rows == row_index[None]
    by_col = jnp.transpose(dense, (0, 2, 1, 3))
    chosen = jnp.where(hit[:, :, :, None, None], by_col[:, :, None], 0.0)
    return jnp.sum(chosen, axis=0)


def group_size(axis):
    if isinstance(axis, tuple):
        size = 1
        for name in axis:
            size *= lax.axis_size(name)
        return size
    return lax.axis_size(axis)


def butterfly_sum(value, axis):
    size = group_size(axis)
    step = 1
    while step < size:
        value = value + lax.ppermute(value, axis, [(i, i ^ step) for i in range(size)])
        step *= 2
    return value


def gather_rows(value):
    chips = lax.axis_size("chip")
    spread = jnp.broadcast_to(value[None], (chips,) + value.shape)
    mine = lax.all_to_all(spread, "chip", 0, 0, tiled=False)
    other = lax.ppermute(mine, "core", [(0, 1), (1, 0)])
    first = lax.axis_index("core") == 0
    pair = jnp.stack([jnp.where(first, mine, other), jnp.where(first, other, mine)], 1)
    return pair.reshape((-1,) + value.shape[1:])


def pair_rows(left, product):
    chips = lax.axis_size("chip")
    parts = left.reshape((chips, 2, -1) + left.shape[1:])
    first = lax.axis_index("core") == 0
    keep_in = jnp.where(first, parts[:, 0], parts[:, 1]).reshape((-1,) + left.shape[1:])
    give_in = jnp.where(first, parts[:, 1], parts[:, 0]).reshape((-1,) + left.shape[1:])
    give = product(give_in).astype(jnp.bfloat16)
    got = lax.ppermute(give, "core", [(0, 1), (1, 0)])
    keep = product(keep_in).astype(jnp.bfloat16)
    pair = keep.astype(jnp.float32) + got.astype(jnp.float32)
    return pair.astype(jnp.bfloat16).reshape((chips, -1) + pair.shape[1:])


def sum_rows(left, product):
    received = lax.all_to_all(pair_rows(left, product), "chip", 0, 0, tiled=False)
    return jnp.sum(received.astype(jnp.float32), axis=0)


def split_three(value):
    high = value.astype(jnp.bfloat16)
    rest = value - high.astype(jnp.float32)
    middle = rest.astype(jnp.bfloat16)
    low = (rest - middle.astype(jnp.float32)).astype(jnp.bfloat16)
    return jnp.stack([high, middle, low])


def join_three(pieces):
    pieces = pieces.astype(jnp.float32)
    return pieces[..., 0] + pieces[..., 1] + pieces[..., 2]


def with_row(rows, pieces):
    extra = jnp.zeros((1, rows.shape[1]), rows.dtype).at[0, : pieces.shape[0]].set(pieces)
    return jnp.concatenate([rows, extra], axis=0)


def body(tokens, target, probe_vector, weight_in, weight_out, slot_rows, slot_count):
    columns, unit, slots, block, width_two = weight_in.shape
    features = tokens.shape[1]
    feature_blocks = features // block
    hidden_width = columns * block
    row_index = slot_rows[:, 0]
    in_use = lax.broadcasted_iota(jnp.int32, (columns, slots), 1) < slot_count[:, 0][:, None]
    mask_low = in_use.astype(jnp.bfloat16)[:, :, None, None]
    mask_full = in_use.astype(jnp.float32)[:, :, None, None]
    tiles_in = weight_in[:, 0] * mask_low
    tiles_out = weight_out[:, 0] * mask_low
    chosen = jnp.take(
        probe_vector.reshape(feature_blocks, block), row_index.reshape(-1), axis=0
    ).reshape(columns, slots, block)
    image_part = jnp.einsum(
        "jsk,jskn->jn", chosen, tiles_in.astype(jnp.float32), precision=lax.Precision.HIGHEST
    )
    x_full = gather_rows(tokens)
    image_and_norm = butterfly_sum(
        jnp.concatenate([image_part.reshape(-1), jnp.sum(probe_vector * probe_vector)[None]]), "blk"
    )
    image = image_and_norm[:-1].reshape(image_part.shape)
    norm_probe = image_and_norm[-1]
    norm_image = butterfly_sum(jnp.sum(image * image)[None], WIDE)[0]
    spectral = jnp.sqrt(norm_image / norm_probe)
    w1 = spread_tiles(tiles_in, row_index, feature_blocks).reshape(features, hidden_width)
    w2 = jnp.transpose(spread_tiles(tiles_out, row_index, feature_blocks), (2, 1, 0, 3)).reshape(
        hidden_width, features
    )
    pre_part = jnp.dot(x_full, w1, preferred_element_type=jnp.float32)
    pre_own = lax.psum_scatter(
        pre_part.astype(jnp.bfloat16), "blk", scatter_dimension=0, tiled=True
    ).astype(jnp.float32)
    pre_own, spectral = lax.optimization_barrier((pre_own, spectral))
    hidden_own = pre_own / spectral
    active_own = activate(hidden_own).astype(jnp.bfloat16)
    active_full = lax.all_gather(active_own, "blk", axis=0, tiled=True)
    outputs = sum_rows(
        active_full, lambda rows: jnp.dot(rows, w2, preferred_element_type=jnp.float32)
    ).astype(jnp.bfloat16)
    residual = (outputs.astype(jnp.float32) - target.astype(jnp.float32)).astype(jnp.bfloat16)
    error_full = gather_rows(residual)
    back_part = lax.dot_general(
        error_full, w2, (((1,), (1,)), ((), ())), preferred_element_type=jnp.float32
    )
    back_own = lax.psum_scatter(
        back_part.astype(jnp.bfloat16), "blk", scatter_dimension=0, tiled=True
    ).astype(jnp.float32)
    g2 = lax.dot_general(
        error_full, active_full, (((0,), (0,)), ((), ())), preferred_element_type=jnp.float32
    )
    grad_out = pick_tiles(g2.reshape(feature_blocks, block, columns, block), row_index) * mask_full
    grad_out = jnp.transpose(grad_out, (0, 1, 3, 2))
    back_own, grad_out = lax.optimization_barrier((back_own, grad_out))
    slope_own = (back_own * activate_slope(hidden_own)).astype(jnp.bfloat16)
    curvature_part = jnp.sum(slope_own.astype(jnp.float32) * pre_own)
    slope_rows = lax.all_gather(
        with_row(slope_own, split_three(curvature_part)), "blk", axis=0, tiled=False
    )
    slope_full = slope_rows[:, :-1].reshape(-1, slope_own.shape[1])
    curvature_blk = jnp.sum(join_three(slope_rows[:, -1, :3]))
    in_rows = pair_rows(
        slope_full,
        lambda rows: lax.dot_general(
            rows, w1, (((1,), (1,)), ((), ())), preferred_element_type=jnp.float32
        ),
    )
    curvature_chip = curvature_blk + lax.ppermute(curvature_blk, "core", [(0, 1), (1, 0)])
    extra = (
        jnp.zeros((in_rows.shape[0], 1, features), jnp.bfloat16)
        .at[:, 0, :3]
        .set(split_three(curvature_chip)[None])
    )
    received = lax.all_to_all(jnp.concatenate([in_rows, extra], axis=1), "chip", 0, 0, tiled=False)
    token_grad = (jnp.sum(received[:, :-1].astype(jnp.float32), axis=0) / spectral).astype(
        jnp.bfloat16
    )
    curvature = jnp.sum(join_three(received[:, -1, :3]))
    g1 = lax.dot_general(
        x_full, slope_full, (((0,), (0,)), ((), ())), preferred_element_type=jnp.float32
    )
    raw_in = pick_tiles(g1.reshape(feature_blocks, block, columns, block), row_index) * mask_full
    outer = jnp.einsum("jsk,jn->jskn", chosen, image) * mask_full
    grad_in = raw_in / spectral - curvature / (spectral**3 * norm_probe) * outer
    return (outputs, token_grad, grad_in[:, None], grad_out[:, None])


def solution(mesh):
    wide, blk = (mesh.shape["wide"], mesh.shape["blk"])
    split = Mesh(mesh.devices.reshape(wide // 2, 2, blk), ("chip", "core", "blk"))
    in_specs = (
        P(WIDE, "blk"),
        P(WIDE, "blk"),
        P("blk"),
        P(WIDE, "blk", None, None, None),
        P(WIDE, "blk", None, None, None),
        P(WIDE, "blk", None),
        P(WIDE, "blk"),
    )
    out_specs = (
        P(WIDE, "blk"),
        P(WIDE, "blk"),
        P(WIDE, "blk", None, None, None),
        P(WIDE, "blk", None, None, None),
    )
    return jax.shard_map(body, mesh=split, in_specs=in_specs, out_specs=out_specs, check_vma=False)
```

profile of v0, /device:TPU:32, one launch (start us, length us, event | category | flops | bytes accessed | tf_op | source)
XLA Modules:
  0.0 324.5 jit_solution(9153554988454920634)
XLA Ops:
  9.1 7.0 %all-to-all-start = ((bf16[16,32,1024]{2,1,0:T(8,128)(2,1)}), bf16[16,32,1024]{2,1,0:T(8,128)(2,1)S(1)}, u32[]{:S(2)}, u32[]{:S(2)}) async-start(bf16[16,32,1024]{2,1,0:T(8,128)(2,1)} %broadcast_in_dim.148), calls=%async_computation | async-start | bytes 2097152 | tf_op jit(solution)/shard_map/all_to_all | solution.py:57
  16.3 17.6 %all-to-all-done = bf16[16,32,1024]{2,1,0:T(8,128)(2,1)S(1)} async-done(((bf16[16,32,1024]{2,1,0:T(8,128)(2,1)}), bf16[16,32,1024]{2,1,0:T(8,128)(2,1)S(1)}, u32[]{:S(2)}, u32[]{:S(2)}) %all-to-all-start) | async-done | bytes 1048608 | tf_op jit(solution)/shard_map/all_to_all | solution.py:57
  38.8 3.7 %fusion.12 = bf16[1024,1024]{1,0:T(8,128)(2,1)} fusion(bf16[1024,1024]{1,0:T(8,128)(2,1)S(1)} %bitcast.166, bf16[128,8,8,128]{3,2,1,0:T(8,128)(2,1)S(1)} %bitcast.173), kind=kOutput, calls=%fused_computation.24 | convolution fusion | flops 2148532224 | bytes 6291456 | tf_op jit(solution)/shard_map/dot_general | solution.py:129
  45.6 3.5 %collective-permute-done.1 = f32[1025]{0:T(1024)S(1)} collective-permute-done((f32[1025]{0:T(1024)S(1)}, f32[1025]{0:T(1024)S(1)}, u32[]{:S(2)}, u32[]{:S(2)}) %collective-permute-start.1) | collective-permute-done | bytes 4132 | tf_op jit(solution)/shard_map/ppermute | solution.py:49
  49.8 3.4 %collective-permute-start.2 = (f32[1025]{0:T(1024)S(1)}, f32[1025]{0:T(1024)S(1)}, u32[]{:S(2)}, u32[]{:S(2)}) collective-permute-start(f32[1025]{0:T(1024)S(1)} %fusion.63), channel_id=1, source_target_pairs={{0,2},{1,3},{2,0},{3,1},{4,6},{5,7},{6,4},{7,5},{8,10},{9,11},{10,... | collective-permute-start | bytes 12308 | tf_op jit(solution)/shard_map/ppermute | solution.py:49
  54.8 6.0 %collective-permute-start.3 = (f32[1025]{0:T(1024)S(1)}, f32[1025]{0:T(1024)S(1)}, u32[]{:S(2)}, u32[]{:S(2)}) collective-permute-start(f32[1025]{0:T(1024)S(1)} %add.135), channel_id=1, source_target_pairs={{0,4},{1,5},{2,6},{3,7},{4,0},{5,1},{6,2},{7,3},{8,12},{9,13},{10,... | collective-permute-start | bytes 12308 | tf_op jit(solution)/shard_map/ppermute | solution.py:49
  72.8 3.1 collective-permute-done.6
  82.9 3.3 %collective-permute-done.8 = f32[1]{0:T(128)} collective-permute-done((f32[1]{0:T(128)}, f32[1]{0:T(128)}, u32[]{:S(2)}, u32[]{:S(2)}) %collective-permute-start.8) | collective-permute-done | bytes 36 | tf_op jit(solution)/shard_map/ppermute | solution.py:49
  90.4 38.5 %all-gather.5.cloned.1.call-done = bf16[1024,1024]{1,0:T(8,128)(2,1)} async-done(((bf16[128,1024]{1,0:T(8,128)(2,1)}), bf16[1024,1024]{1,0:T(8,128)(2,1)}) %all-gather.5.cloned.1.call-update) | async-done | bytes 2097168 | tf_op jit(solution)/shard_map/all_gather | solution.py:136
  132.1 2.6 collective-permute-done.9
  136.0 24.1 %all_to_all.20 = bf16[16,32,1024]{2,1,0:T(8,128)(2,1)S(1)} all-to-all(bf16[16,32,1024]{2,1,0:T(8,128)(2,1)S(1)} %bitcast.189), channel_id=1, replica_groups=mesh['chip'=16,'core'=2,'blk'=8] {'chip'}, dimensions={0} | all-to-all | bytes 2097152 | tf_op jit(solution)/shard_map/all_to_all | solution.py:78
  160.6 19.5 %all_to_all.21 = bf16[16,32,1024]{2,1,0:T(8,128)(2,1)S(1)} all-to-all(bf16[16,32,1024]{2,1,0:T(8,128)(2,1)S(1)} %broadcast_in_dim.172), channel_id=1, replica_groups=mesh['chip'=16,'core'=2,'blk'=8] {'chip'}, dimensions={0} | all-to-all | bytes 2097152 | tf_op jit(solution)/shard_map/all_to_all | solution.py:57
  180.1 2.7 collective-permute-done.10
  185.4 3.7 %fusion.15 = bf16[1024,1024]{1,0:T(8,128)(2,1)} fusion(bf16[1024,1024]{1,0:T(8,128)(2,1)S(1)} %bitcast.170, bf16[128,8,8,128]{3,2,1,0:T(8,128)(2,1)S(1)} %bitcast.178), kind=kOutput, calls=%fused_computation.25 | convolution fusion | flops 2148532224 | bytes 6291456 | tf_op jit(solution)/shard_map/dot_general | solution.py:142
  193.3 4.1 %copy.88 = bf16[1024,1024]{1,0:T(8,128)(2,1)} copy(bf16[1024,1024]{0,1:T(8,128)(2,1)} %bitcast.171) | data formatting | bytes 4194304 | tf_op jit(solution)/shard_map/dot_general | solution.py:148
  197.5 4.0 %convolution_bitcast_fusion.1 = f32[8,8,128,128]{3,2,1,0:T(8,128)S(1)} fusion(bf16[8,128,1024,1]{2,1,3,0:T(8,128)(2,1)} %bitcast.181, bf16[8,128,1024,1]{2,1,0,3:T(8,128)(2,1)S(1)} %bitcast.180), kind=kOutput, calls=%fused_computation.4 | convolution fusion | flops 2147483648 | bytes 8388608 | tf_op jit(solution)/shard_map/dot_general | solution.py:148
  203.5 23.0 %reduce-scatter.5.cloned.1.call-done = bf16[128,1024]{1,0:T(8,128)(2,1)} async-done(((bf16[1024,1024]{1,0:T(8,128)(2,1)}), bf16[128,1024]{1,0:T(8,128)(2,1)}) %reduce-scatter.5.cloned.1.call-update) | async-done | bytes 262160 | tf_op jit(solution)/shard_map/reduce_scatter | solution.py:145
  231.3 40.6 %all-gather.7.cloned.1.call-done = bf16[8,129,1024]{2,1,0:T(8,128)(2,1)} async-done(((bf16[1,129,1024]{2,1,0:T(8,128)(2,1)}), bf16[8,129,1024]{2,1,0:T(8,128)(2,1)}) %all-gather.7.cloned.1.call-update) | async-done | bytes 2113552 | tf_op jit(solution)/shard_map/all_gather | solution.py:156
  282.0 3.1 add_convert_fusion
  286.4 6.8 %all-to-all-start.3 = ((bf16[16,33,1024]{2,1,0:T(8,128)(2,1)}), bf16[16,33,1024]{2,1,0:T(8,128)(2,1)S(1)}, u32[]{:S(2)}, u32[]{:S(2)}) async-start(bf16[16,33,1024]{2,1,0:T(8,128)(2,1)} %pad_maximum_fusion.2), calls=%async_computation.5 | async-start | bytes 2621440 | tf_op jit(solution)/shard_map/all_to_all | solution.py:173
  293.2 4.0 %copy.91 = bf16[1024,1024]{1,0:T(8,128)(2,1)} copy(bf16[1024,1024]{0,1:T(8,128)(2,1)} %bitcast.167) | data formatting | bytes 4194304 | tf_op jit(solution)/shard_map/dot_general | solution.py:178
  300.4 2.6 copy.92
  303.0 4.6 %convolution_bitcast_fusion = f32[8,8,128,128]{3,2,1,0:T(8,128)S(1)} fusion(bf16[8,128,1024,1]{2,1,3,0:T(8,128)(2,1)} %bitcast.179, bf16[8,128,1024,1]{2,1,0,3:T(8,128)(2,1)} %bitcast.182), kind=kOutput, calls=%fused_computation.3 | convolution fusion | flops 2147483648 | bytes 8388608 | tf_op jit(solution)/shard_map/dot_general | solution.py:178
  308.6 5.8 %all-to-all-done.3 = bf16[16,33,1024]{2,1,0:T(8,128)(2,1)S(1)} async-done(((bf16[16,33,1024]{2,1,0:T(8,128)(2,1)}), bf16[16,33,1024]{2,1,0:T(8,128)(2,1)S(1)}, u32[]{:S(2)}, u32[]{:S(2)}) %all-to-all-start.3) | async-done | bytes 1081376 | tf_op jit(solution)/shard_map/all_to_all | solution.py:173
  (125 shorter events, 64.4 us)
Async XLA Ops:
  7.2 9.0 %copy-start.13 = (s32[8,1]{0,1:T(1,128)S(1)}, s32[8,1]{0,1:T(1,128)}, u32[]{:S(2)}) copy-start(s32[8,1]{0,1:T(1,128)} %param.17) | copy-start | bytes 100
  9.1 24.7 %all-to-all-start = ((bf16[16,32,1024]{2,1,0:T(8,128)(2,1)}), bf16[16,32,1024]{2,1,0:T(8,128)(2,1)S(1)}, u32[]{:S(2)}, u32[]{:S(2)}) async-start(bf16[16,32,1024]{2,1,0:T(8,128)(2,1)} %broadcast_in_dim.148), calls=%async_computation | async-start | bytes 2097152 | tf_op jit(solution)/shard_map/all_to_all | solution.py:57
  16.2 71.4 %reduce-scatter.3.cloned.1.call-start = ((), (), s32[]{:S(2)}) async-start(), calls=%async_computation.6 | async-start | bytes 2359296 | tf_op jit(solution)/shard_map/reduce_scatter | solution.py:130
  33.9 3.0 collective-permute-start
  42.5 47.3 %copy-start.9 = (bf16[8,128,128]{2,1,0:T(8,128)(2,1)S(1)}, bf16[8,128,128]{2,1,0:T(8,128)(2,1)}, u32[]{:S(2)}) copy-start(bf16[8,128,128]{2,1,0:T(8,128)(2,1)} %get-tuple-element.63) | copy-start | bytes 786436
  42.5 86.4 %all-gather.5.cloned.1.call-start = ((), (), s32[]{:S(2)}) async-start(), calls=%async_computation.7 | async-start | bytes 2359296 | tf_op jit(solution)/shard_map/all_gather | solution.py:136
  45.4 3.7 %collective-permute-start.1 = (f32[1025]{0:T(1024)S(1)}, f32[1025]{0:T(1024)S(1)}, u32[]{:S(2)}, u32[]{:S(2)}) collective-permute-start(f32[1025]{0:T(1024)S(1)} %pad_maximum_fusion.3), channel_id=1, source_target_pairs={{0,1},{1,0},{2,3},{3,2},{4,5},{5,4},{6,7},{7,6},{8,9},{9,8},{10,11... | collective-permute-start | bytes 12308 | tf_op jit(solution)/shard_map/ppermute | solution.py:49
  49.8 5.0 %collective-permute-start.2 = (f32[1025]{0:T(1024)S(1)}, f32[1025]{0:T(1024)S(1)}, u32[]{:S(2)}, u32[]{:S(2)}) collective-permute-start(f32[1025]{0:T(1024)S(1)} %fusion.63), channel_id=1, source_target_pairs={{0,2},{1,3},{2,0},{3,1},{4,6},{5,7},{6,4},{7,5},{8,10},{9,11},{10,... | collective-permute-start | bytes 12308 | tf_op jit(solution)/shard_map/ppermute | solution.py:49
  54.8 7.7 %collective-permute-start.3 = (f32[1025]{0:T(1024)S(1)}, f32[1025]{0:T(1024)S(1)}, u32[]{:S(2)}, u32[]{:S(2)}) collective-permute-start(f32[1025]{0:T(1024)S(1)} %add.135), channel_id=1, source_target_pairs={{0,4},{1,5},{2,6},{3,7},{4,0},{5,1},{6,2},{7,3},{8,12},{9,13},{10,... | collective-permute-start | bytes 12308 | tf_op jit(solution)/shard_map/ppermute | solution.py:49
  63.7 1.4 collective-permute-start.4
  66.3 3.7 %collective-permute-start.5 = (f32[1]{0:T(128)}, f32[1]{0:T(128)}, u32[]{:S(2)}, u32[]{:S(2)}) collective-permute-start(f32[1]{0:T(128)} %add.137), channel_id=1, source_target_pairs={{0,16},{8,24},{16,0},{24,8},{32,48},{40,56},{48,32},{56,40},{64,80... | collective-permute-start | bytes 20 | tf_op jit(solution)/shard_map/ppermute | solution.py:49
  70.7 5.2 %collective-permute-start.6 = (f32[1]{0:T(128)}, f32[1]{0:T(128)}, u32[]{:S(2)}, u32[]{:S(2)}) collective-permute-start(f32[1]{0:T(128)} %add.138), channel_id=1, source_target_pairs={{0,32},{8,40},{16,48},{24,56},{32,0},{40,8},{48,16},{56,24},{64,96... | collective-permute-start | bytes 20 | tf_op jit(solution)/shard_map/ppermute | solution.py:49
  76.6 3.7 %collective-permute-start.7 = (f32[1]{0:T(128)}, f32[1]{0:T(128)}, u32[]{:S(2)}, u32[]{:S(2)}) collective-permute-start(f32[1]{0:T(128)} %add.139), channel_id=1, source_target_pairs={{0,64},{8,72},{16,80},{24,88},{32,96},{40,104},{48,112},{56,120},{... | collective-permute-start | bytes 20 | tf_op jit(solution)/shard_map/ppermute | solution.py:49
  80.9 5.2 %collective-permute-start.8 = (f32[1]{0:T(128)}, f32[1]{0:T(128)}, u32[]{:S(2)}, u32[]{:S(2)}) collective-permute-start(f32[1]{0:T(128)} %add.140), channel_id=1, source_target_pairs={{0,128},{8,136},{16,144},{24,152},{32,160},{40,168},{48,176},{56,1... | collective-permute-start | bytes 20 | tf_op jit(solution)/shard_map/ppermute | solution.py:49
  89.5 137.0 %reduce-scatter.5.cloned.1.call-start = ((), (), s32[]{:S(2)}) async-start(), calls=%async_computation.8 | async-start | bytes 2359296 | tf_op jit(solution)/shard_map/reduce_scatter | solution.py:145
  90.4 44.4 %copy-start.5 = (bf16[8,128,8,128]{3,2,1,0:T(8,128)(2,1)}, bf16[8,128,8,128]{3,2,1,0:T(8,128)(2,1)S(1)}, u32[]{:S(2)}) copy-start(bf16[8,128,8,128]{3,2,1,0:T(8,128)(2,1)S(1)} %select_add_fusion) | copy-start | bytes 6291460
  131.8 2.9 collective-permute-start.9
  136.0 24.4 %copy-start.11 = (bf16[32,1024]{1,0:T(8,128)(2,1)S(1)}, bf16[32,1024]{1,0:T(8,128)(2,1)}, u32[]{:S(2)}) copy-start(bf16[32,1024]{1,0:T(8,128)(2,1)} %param.12) | copy-start | bytes 196612
  160.4 22.5 %copy-start.10 = (bf16[32,1024]{1,0:T(8,128)(2,1)}, bf16[32,1024]{1,0:T(8,128)(2,1)S(1)}, u32[]{:S(2)}) copy-start(bf16[32,1024]{1,0:T(8,128)(2,1)S(1)} %reduce_sum.86) | copy-start | bytes 196612
  180.1 2.7 collective-permute-start.10
  189.2 82.7 %all-gather.7.cloned.1.call-start = ((), (), s32[]{:S(2)}) async-start(), calls=%async_computation.9 | async-start | bytes 2506752 | tf_op jit(solution)/shard_map/all_gather | solution.py:156
  277.6 4.4 %collective-permute-start.11 = (bf16[512,1024]{1,0:T(8,128)(2,1)}, bf16[512,1024]{1,0:T(8,128)(2,1)}, u32[]{:S(2)}, u32[]{:S(2)}) collective-permute-start(bf16[512,1024]{1,0:T(8,128)(2,1)} %fusion.27), channel_id=1, source_target_pairs={{0,8},{8,0},{1,9},{9,1},{2,10},{10,2},{3,11},{11,3},{4,12},{12,4},... | collective-permute-start | bytes 3145736 | tf_op jit(solution)/shard_map/ppermute | solution.py:71
  279.1 1.6 collective-permute-start.12
  286.4 28.0 %all-to-all-start.3 = ((bf16[16,33,1024]{2,1,0:T(8,128)(2,1)}), bf16[16,33,1024]{2,1,0:T(8,128)(2,1)S(1)}, u32[]{:S(2)}, u32[]{:S(2)}) async-start(bf16[16,33,1024]{2,1,0:T(8,128)(2,1)} %pad_maximum_fusion.2), calls=%async_computation.5 | async-start | bytes 2621440 | tf_op jit(solution)/shard_map/all_to_all | solution.py:173
  (9 other events, 15.8 us)
Sparse Core Ops, SparseCore 0:
  42.6 40.4 reduce-scatter.2
  89.6 39.2 all-gather.4
  189.3 37.1 reduce-scatter.4
  231.4 40.4 all-gather.6
where the time goes:
time: 326 us; the launch traced here: 324 us
  waiting for transfers between devices  151 us (46%)
  blocking collectives  43.7 us (13%)
  starting transfers between devices  31.9 us (10%)
  local copies, waits for them, and re-layouts  30 us (9%)
  matrix products  24.2 us (7%)
  between operations  22.7 us (7%)
  other arithmetic  21.4 us (7%)
    all_gather x1, waiting for transfers between devices, body(): lax.all_gather(with_row(slope_own, split_three(curvature_part)), 'blk', a...  40.6 us
    all_gather x1, waiting for transfers between devices, body(): active_full = lax.all_gather(active_own, 'blk', axis=0, tiled=True)  38.5 us
    all_to_all x1, blocking collectives, sum_rows(): lax.all_to_all(pair_rows(left, product), 'chip', 0, 0, tiled=False)  24.1 us
    reduce_scatter x1, waiting for transfers between devices, body(): lax.psum_scatter(back_part.astype(jnp.bfloat16), 'blk', scatter_dimension...  23 us
    all_to_all x1, blocking collectives, gather_rows(): mine = lax.all_to_all(spread, 'chip', 0, 0, tiled=False)  19.5 us
    ppermute x8, waiting for transfers between devices, butterfly_sum(): lax.ppermute(value, axis, [(i, i ^ step) for i in range(size)])  18.7 us
    all_to_all x1, waiting for transfers between devices, gather_rows(): mine = lax.all_to_all(spread, 'chip', 0, 0, tiled=False)  17.6 us
    ppermute x8, starting transfers between devices, butterfly_sum(): lax.ppermute(value, axis, [(i, i ^ step) for i in range(size)])  17.1 us
  transfers between devices with their start and end apart: 19, of which 16 were waited for; matrix products, arithmetic and copies ran while one was open for 12% of the time, Pallas kernels for 0%

commit v1 on v0

--- a/solution.py
+++ b/solution.py
@@ -133,7 +133,13 @@
     pre_own, spectral = lax.optimization_barrier((pre_own, spectral))
     hidden_own = pre_own / spectral
     active_own = activate(hidden_own).astype(jnp.bfloat16)
-    active_full = lax.all_gather(active_own, "blk", axis=0, tiled=True)
+    _obtain_strings = lambda array_here: jnp.concatenate(
+        lax.all_to_all(
+            jnp.stack([array_here for _ in range(lax.axis_size("blk"))], 0), "blk", 0, 0
+        ),
+        0,
+    )
+    active_full = _obtain_strings(active_own)
     outputs = sum_rows(
         active_full, lambda rows: jnp.dot(rows, w2, preferred_element_type=jnp.float32)
     ).astype(jnp.bfloat16)

time: 326 us -> 341 us (1.046)
  starting transfers between devices: 31.9 us -> 40.3 us
  local copies, waits for them, and re-layouts: 30 us -> 35.3 us
  waiting for transfers between devices: 151 us -> 155 us
    all_to_all x0 -> x1, waiting for transfers between devices: none -> 43.6 us  [body(): lax.all_to_all(jnp.stack([array_here for _ in range(lax.axis_size('blk'))...]
    all_gather x1 -> x0, waiting for transfers between devices: 38.5 us -> none  [body(): active_full = lax.all_gather(active_own, 'blk', axis=0, tiled=True)]
    all_to_all x0 -> x1, starting transfers between devices: none -> 8.42 us  [body(): lax.all_to_all(jnp.stack([array_here for _ in range(lax.axis_size('blk'))...]
    unnamed x34 -> x32, local copies, waits for them, and re-layouts: 9.01 us -> 9.78 us
  transfers between devices with their start and end apart: 19 -> 19, of which waited for: 16 -> 16; matrix products, arithmetic and copies ran while one was open for 12% -> 11% of each run, Pallas kernels for 0% -> 0%
where the time goes in v1:
time: 341 us; the launch traced here: 339 us
  waiting for transfers between devices  155 us (45%)
  blocking collectives  41 us (12%)
  starting transfers between devices  40.3 us (12%)
  local copies, waits for them, and re-layouts  35.3 us (10%)
  matrix products  24.2 us (7%)
  between operations  22.2 us (7%)
  other arithmetic  21.7 us (6%)
    all_to_all x1, waiting for transfers between devices, body(): lax.all_to_all(jnp.stack([array_here for _ in range(lax.axis_size('blk'))...  43.6 us
    all_gather x1, waiting for transfers between devices, body(): lax.all_gather(with_row(slope_own, split_three(curvature_part)), 'blk', a...  40.8 us
    reduce_scatter x1, waiting for transfers between devices, body(): lax.psum_scatter(back_part.astype(jnp.bfloat16), 'blk', scatter_dimension...  21.6 us
    all_to_all x1, blocking collectives, sum_rows(): lax.all_to_all(pair_rows(left, product), 'chip', 0, 0, tiled=False)  21.5 us
    all_to_all x1, blocking collectives, gather_rows(): mine = lax.all_to_all(spread, 'chip', 0, 0, tiled=False)  19.5 us
    ppermute x8, waiting for transfers between devices, butterfly_sum(): lax.ppermute(value, axis, [(i, i ^ step) for i in range(size)])  18.6 us
    all_to_all x1, waiting for transfers between devices, gather_rows(): mine = lax.all_to_all(spread, 'chip', 0, 0, tiled=False)  17.6 us
    ppermute x8, starting transfers between devices, butterfly_sum(): lax.ppermute(value, axis, [(i, i ^ step) for i in range(size)])  17.1 us
  transfers between devices with their start and end apart: 19, of which 16 were waited for; matrix products, arithmetic and copies ran while one was open for 11% of the time, Pallas kernels for 0%

profile of v1, /device:TPU:32, one launch (start us, length us, event | category | flops | bytes accessed | tf_op | source)
XLA Modules:
  0.0 339.3 jit_solution(2097227275110595872)
XLA Ops:
  9.1 7.0 %all-to-all-start = ((bf16[16,32,1024]{2,1,0:T(8,128)(2,1)}), bf16[16,32,1024]{2,1,0:T(8,128)(2,1)S(1)}, u32[]{:S(2)}, u32[]{:S(2)}) async-start(bf16[16,32,1024]{2,1,0:T(8,128)(2,1)} %broadcast_in_dim.148), calls=%async_computation | async-start | bytes 2097152 | tf_op jit(solution)/shard_map/all_to_all | solution.py:57
  16.3 17.6 %all-to-all-done = bf16[16,32,1024]{2,1,0:T(8,128)(2,1)S(1)} async-done(((bf16[16,32,1024]{2,1,0:T(8,128)(2,1)}), bf16[16,32,1024]{2,1,0:T(8,128)(2,1)S(1)}, u32[]{:S(2)}, u32[]{:S(2)}) %all-to-all-start) | async-done | bytes 1048608 | tf_op jit(solution)/shard_map/all_to_all | solution.py:57
  38.8 3.7 %fusion.12 = bf16[1024,1024]{1,0:T(8,128)(2,1)} fusion(bf16[1024,1024]{1,0:T(8,128)(2,1)S(1)} %bitcast.170, bf16[128,8,8,128]{3,2,1,0:T(8,128)(2,1)S(1)} %bitcast.175), kind=kOutput, calls=%fused_computation.24 | convolution fusion | flops 2148532224 | bytes 6291456 | tf_op jit(solution)/shard_map/dot_general | solution.py:129
  45.5 3.5 %collective-permute-done.1 = f32[1025]{0:T(1024)S(1)} collective-permute-done((f32[1025]{0:T(1024)S(1)}, f32[1025]{0:T(1024)S(1)}, u32[]{:S(2)}, u32[]{:S(2)}) %collective-permute-start.1) | collective-permute-done | bytes 4132 | tf_op jit(solution)/shard_map/ppermute | solution.py:49
  49.7 3.4 collective-permute-start.2
  54.7 6.0 %collective-permute-start.3 = (f32[1025]{0:T(1024)S(1)}, f32[1025]{0:T(1024)S(1)}, u32[]{:S(2)}, u32[]{:S(2)}) collective-permute-start(f32[1025]{0:T(1024)S(1)} %add.135), channel_id=1, source_target_pairs={{0,4},{1,5},{2,6},{3,7},{4,0},{5,1},{6,2},{7,3},{8,12},{9,13},{10,... | collective-permute-start | bytes 12308 | tf_op jit(solution)/shard_map/ppermute | solution.py:49
  72.6 3.1 collective-permute-done.6
  82.5 3.3 collective-permute-done.8
  90.0 8.4 %all-to-all-start.1 = ((bf16[8,128,1024]{1,2,0:T(8,128)(2,1)}), bf16[8,128,1024]{1,2,0:T(8,128)(2,1)}, u32[]{:S(2)}, u32[]{:S(2)}) async-start(bf16[8,128,1024]{1,2,0:T(8,128)(2,1)} %stack.56), calls=%async_computation.2 | async-start | bytes 4194304 | tf_op jit(solution)/shard_map/all_to_all | solution.py:137
  100.6 43.6 %all-to-all-done.1 = bf16[8,128,1024]{1,2,0:T(8,128)(2,1)} async-done(((bf16[8,128,1024]{1,2,0:T(8,128)(2,1)}), bf16[8,128,1024]{1,2,0:T(8,128)(2,1)}, u32[]{:S(2)}, u32[]{:S(2)}) %all-to-all-start.1) | async-done | bytes 2097184 | tf_op jit(solution)/shard_map/all_to_all | solution.py:137
  144.2 2.9 copy.130
  154.1 21.5 %all_to_all.25 = bf16[16,32,1024]{2,1,0:T(8,128)(2,1)} all-to-all(bf16[16,32,1024]{2,1,0:T(8,128)(2,1)S(1)} %bitcast.191), channel_id=1, replica_groups=mesh['chip'=16,'core'=2,'blk'=8] {'chip'}, dimensions={0} | all-to-all | bytes 2097152 | tf_op jit(solution)/shard_map/all_to_all | solution.py:78
  177.3 19.5 %all_to_all.26 = bf16[16,32,1024]{2,1,0:T(8,128)(2,1)S(1)} all-to-all(bf16[16,32,1024]{2,1,0:T(8,128)(2,1)S(1)} %broadcast_in_dim.172), channel_id=1, replica_groups=mesh['chip'=16,'core'=2,'blk'=8] {'chip'}, dimensions={0} | all-to-all | bytes 2097152 | tf_op jit(solution)/shard_map/all_to_all | solution.py:57
  196.8 2.7 collective-permute-done.10
  202.1 3.7 %fusion.15 = bf16[1024,1024]{1,0:T(8,128)(2,1)} fusion(bf16[1024,1024]{1,0:T(8,128)(2,1)S(1)} %bitcast.172, bf16[128,8,8,128]{3,2,1,0:T(8,128)(2,1)S(1)} %bitcast.180), kind=kOutput, calls=%fused_computation.25 | convolution fusion | flops 2148532224 | bytes 6291456 | tf_op jit(solution)/shard_map/dot_general | solution.py:148
  209.3 4.1 %copy.135 = bf16[1024,1024]{1,0:T(8,128)(2,1)} copy(bf16[1024,1024]{0,1:T(8,128)(2,1)} %bitcast.173) | data formatting | bytes 4194304 | tf_op jit(solution)/shard_map/dot_general | solution.py:154
  213.4 4.0 %convolution_bitcast_fusion.1 = f32[8,8,128,128]{3,2,1,0:T(8,128)S(1)} fusion(bf16[8,128,1024,1]{2,1,3,0:T(8,128)(2,1)} %bitcast.183, bf16[8,128,1024,1]{2,1,0,3:T(8,128)(2,1)S(1)} %bitcast.182), kind=kOutput, calls=%fused_computation.4 | convolution fusion | flops 2147483648 | bytes 8388608 | tf_op jit(solution)/shard_map/dot_general | solution.py:154
  219.5 21.6 %reduce-scatter.5.cloned.1.call-done = bf16[128,1024]{1,0:T(8,128)(2,1)} async-done(((bf16[1024,1024]{1,0:T(8,128)(2,1)}), bf16[128,1024]{1,0:T(8,128)(2,1)}) %reduce-scatter.5.cloned.1.call-update) | async-done | bytes 262160 | tf_op jit(solution)/shard_map/reduce_scatter | solution.py:151
  245.9 40.8 %all-gather.4.cloned.1.call-done = bf16[8,129,1024]{2,1,0:T(8,128)(2,1)} async-done(((bf16[1,129,1024]{2,1,0:T(8,128)(2,1)}), bf16[8,129,1024]{2,1,0:T(8,128)(2,1)}) %all-gather.4.cloned.1.call-update) | async-done | bytes 2113552 | tf_op jit(solution)/shard_map/all_gather | solution.py:162
  296.9 3.1 add_convert_fusion
  301.3 6.8 %all-to-all-start.4 = ((bf16[16,33,1024]{2,1,0:T(8,128)(2,1)}), bf16[16,33,1024]{2,1,0:T(8,128)(2,1)S(1)}, u32[]{:S(2)}, u32[]{:S(2)}) async-start(bf16[16,33,1024]{2,1,0:T(8,128)(2,1)} %pad_maximum_fusion.2), calls=%async_computation.6 | async-start | bytes 2621440 | tf_op jit(solution)/shard_map/all_to_all | solution.py:179
  308.1 4.0 %copy.139 = bf16[1024,1024]{1,0:T(8,128)(2,1)} copy(bf16[1024,1024]{0,1:T(8,128)(2,1)} %bitcast.171) | data formatting | bytes 4194304 | tf_op jit(solution)/shard_map/dot_general | solution.py:184
  317.7 4.6 %convolution_bitcast_fusion = f32[8,8,128,128]{3,2,1,0:T(8,128)S(1)} fusion(bf16[8,128,1024,1]{2,1,3,0:T(8,128)(2,1)} %bitcast.181, bf16[8,128,1024,1]{2,1,0,3:T(8,128)(2,1)} %bitcast.184), kind=kOutput, calls=%fused_computation.3 | convolution fusion | flops 2147483648 | bytes 8388608 | tf_op jit(solution)/shard_map/dot_general | solution.py:184
  323.3 5.9 %all-to-all-done.4 = bf16[16,33,1024]{2,1,0:T(8,128)(2,1)S(1)} async-done(((bf16[16,33,1024]{2,1,0:T(8,128)(2,1)}), bf16[16,33,1024]{2,1,0:T(8,128)(2,1)S(1)}, u32[]{:S(2)}, u32[]{:S(2)}) %all-to-all-start.4) | async-done | bytes 1081376 | tf_op jit(solution)/shard_map/all_to_all | solution.py:179
  (125 shorter events, 72.3 us)
Async XLA Ops:
  7.2 9.0 %copy-start.12 = (s32[8,1]{0,1:T(1,128)S(1)}, s32[8,1]{0,1:T(1,128)}, u32[]{:S(2)}) copy-start(s32[8,1]{0,1:T(1,128)} %param.17) | copy-start | bytes 100
  9.1 24.7 %all-to-all-start = ((bf16[16,32,1024]{2,1,0:T(8,128)(2,1)}), bf16[16,32,1024]{2,1,0:T(8,128)(2,1)S(1)}, u32[]{:S(2)}, u32[]{:S(2)}) async-start(bf16[16,32,1024]{2,1,0:T(8,128)(2,1)} %broadcast_in_dim.148), calls=%async_computation | async-start | bytes 2097152 | tf_op jit(solution)/shard_map/all_to_all | solution.py:57
  16.2 70.9 %reduce-scatter.3.cloned.1.call-start = ((), (), s32[]{:S(2)}) async-start(), calls=%async_computation.7 | async-start | bytes 2359296 | tf_op jit(solution)/shard_map/reduce_scatter | solution.py:130
  33.9 3.0 collective-permute-start
  45.3 3.7 %collective-permute-start.1 = (f32[1025]{0:T(1024)S(1)}, f32[1025]{0:T(1024)S(1)}, u32[]{:S(2)}, u32[]{:S(2)}) collective-permute-start(f32[1025]{0:T(1024)S(1)} %pad_maximum_fusion.3), channel_id=1, source_target_pairs={{0,1},{1,0},{2,3},{3,2},{4,5},{5,4},{6,7},{7,6},{8,9},{9,8},{10,11... | collective-permute-start | bytes 12308 | tf_op jit(solution)/shard_map/ppermute | solution.py:49
  49.7 5.0 %collective-permute-start.2 = (f32[1025]{0:T(1024)S(1)}, f32[1025]{0:T(1024)S(1)}, u32[]{:S(2)}, u32[]{:S(2)}) collective-permute-start(f32[1025]{0:T(1024)S(1)} %fusion.63), channel_id=1, source_target_pairs={{0,2},{1,3},{2,0},{3,1},{4,6},{5,7},{6,4},{7,5},{8,10},{9,11},{10,... | collective-permute-start | bytes 12308 | tf_op jit(solution)/shard_map/ppermute | solution.py:49
  54.7 7.7 %collective-permute-start.3 = (f32[1025]{0:T(1024)S(1)}, f32[1025]{0:T(1024)S(1)}, u32[]{:S(2)}, u32[]{:S(2)}) collective-permute-start(f32[1025]{0:T(1024)S(1)} %add.135), channel_id=1, source_target_pairs={{0,4},{1,5},{2,6},{3,7},{4,0},{5,1},{6,2},{7,3},{8,12},{9,13},{10,... | collective-permute-start | bytes 12308 | tf_op jit(solution)/shard_map/ppermute | solution.py:49
  63.6 1.4 collective-permute-start.4
  66.2 3.7 %collective-permute-start.5 = (f32[1]{0:T(128)}, f32[1]{0:T(128)}, u32[]{:S(2)}, u32[]{:S(2)}) collective-permute-start(f32[1]{0:T(128)} %add.137), channel_id=1, source_target_pairs={{0,16},{8,24},{16,0},{24,8},{32,48},{40,56},{48,32},{56,40},{64,80... | collective-permute-start | bytes 20 | tf_op jit(solution)/shard_map/ppermute | solution.py:49
  70.5 5.2 %collective-permute-start.6 = (f32[1]{0:T(128)}, f32[1]{0:T(128)}, u32[]{:S(2)}, u32[]{:S(2)}) collective-permute-start(f32[1]{0:T(128)} %add.138), channel_id=1, source_target_pairs={{0,32},{8,40},{16,48},{24,56},{32,0},{40,8},{48,16},{56,24},{64,96... | collective-permute-start | bytes 20 | tf_op jit(solution)/shard_map/ppermute | solution.py:49
  76.3 3.7 %collective-permute-start.7 = (f32[1]{0:T(128)}, f32[1]{0:T(128)}, u32[]{:S(2)}, u32[]{:S(2)}) collective-permute-start(f32[1]{0:T(128)} %add.139), channel_id=1, source_target_pairs={{0,64},{8,72},{16,80},{24,88},{32,96},{40,104},{48,112},{56,120},{... | collective-permute-start | bytes 20 | tf_op jit(solution)/shard_map/ppermute | solution.py:49
  80.6 5.2 %collective-permute-start.8 = (f32[1]{0:T(128)}, f32[1]{0:T(128)}, u32[]{:S(2)}, u32[]{:S(2)}) collective-permute-start(f32[1]{0:T(128)} %add.140), channel_id=1, source_target_pairs={{0,128},{8,136},{16,144},{24,152},{32,160},{40,168},{48,176},{56,1... | collective-permute-start | bytes 20 | tf_op jit(solution)/shard_map/ppermute | solution.py:49
  90.0 8.6 %copy-start.8 = (bf16[8,128,128]{2,1,0:T(8,128)(2,1)S(1)}, bf16[8,128,128]{2,1,0:T(8,128)(2,1)}, u32[]{:S(2)}) copy-start(bf16[8,128,128]{2,1,0:T(8,128)(2,1)} %get-tuple-element.71) | copy-start | bytes 786436
  90.0 54.2 %all-to-all-start.1 = ((bf16[8,128,1024]{1,2,0:T(8,128)(2,1)}), bf16[8,128,1024]{1,2,0:T(8,128)(2,1)}, u32[]{:S(2)}, u32[]{:S(2)}) async-start(bf16[8,128,1024]{1,2,0:T(8,128)(2,1)} %stack.56), calls=%async_computation.2 | async-start | bytes 4194304 | tf_op jit(solution)/shard_map/all_to_all | solution.py:137
  98.5 142.7 %reduce-scatter.5.cloned.1.call-start = ((), (), s32[]{:S(2)}) async-start(), calls=%async_computation.8 | async-start | bytes 2359296 | tf_op jit(solution)/shard_map/reduce_scatter | solution.py:151
  149.9 2.9 collective-permute-start.9
  154.1 23.0 %copy-start.10 = (bf16[32,1024]{1,0:T(8,128)(2,1)S(1)}, bf16[32,1024]{1,0:T(8,128)(2,1)}, u32[]{:S(2)}) copy-start(bf16[32,1024]{1,0:T(8,128)(2,1)} %param.12) | copy-start | bytes 196612
  177.1 22.5 %copy-start.9 = (bf16[32,1024]{1,0:T(8,128)(2,1)}, bf16[32,1024]{1,0:T(8,128)(2,1)S(1)}, u32[]{:S(2)}) copy-start(bf16[32,1024]{1,0:T(8,128)(2,1)S(1)} %reduce_sum.86) | copy-start | bytes 196612
  196.8 2.7 collective-permute-start.10
  205.9 80.8 %all-gather.4.cloned.1.call-start = ((), (), s32[]{:S(2)}) async-start(), calls=%async_computation.9 | async-start | bytes 2506752 | tf_op jit(solution)/shard_map/all_gather | solution.py:162
  209.3 4.1 %copy-start.6 = (bf16[1024,1024]{1,0:T(8,128)(2,1)S(1)}, bf16[1024,1024]{1,0:T(8,128)(2,1)}, u32[]{:S(2)}) copy-start(bf16[1024,1024]{1,0:T(8,128)(2,1)} %copy.137) | copy-start | bytes 6291460
  292.4 4.4 %collective-permute-start.11 = (bf16[512,1024]{1,0:T(8,128)(2,1)}, bf16[512,1024]{1,0:T(8,128)(2,1)}, u32[]{:S(2)}, u32[]{:S(2)}) collective-permute-start(bf16[512,1024]{1,0:T(8,128)(2,1)} %fusion.27), channel_id=1, source_target_pairs={{0,8},{8,0},{1,9},{9,1},{2,10},{10,2},{3,11},{11,3},{4,12},{12,4},... | collective-permute-start | bytes 3145736 | tf_op jit(solution)/shard_map/ppermute | solution.py:71
  293.9 1.6 collective-permute-start.12
  301.3 28.0 %all-to-all-start.4 = ((bf16[16,33,1024]{2,1,0:T(8,128)(2,1)}), bf16[16,33,1024]{2,1,0:T(8,128)(2,1)S(1)}, u32[]{:S(2)}, u32[]{:S(2)}) async-start(bf16[16,33,1024]{2,1,0:T(8,128)(2,1)} %pad_maximum_fusion.2), calls=%async_computation.6 | async-start | bytes 2621440 | tf_op jit(solution)/shard_map/all_to_all | solution.py:179
  (8 other events, 11.7 us)
Sparse Core Ops, SparseCore 0:
  42.6 40.3 reduce-scatter.2
  206.0 35.0 reduce-scatter.4
  246.0 40.6 all-gather.3
